TPU v7x, 256 devices: a whole 4x4x8 slice. The times are simulated.
256 devices in a mesh: layer: 2 (over core), feat: 4 (over x), tok: 32 (over z, y).
Axes of the slice: x: 4, y: 4, z: 8, core: 2. Of those that a mesh axis runs over, the one named last changes fastest.
Arguments:
- resid_in: bfloat16 [8192, 2304], P('tok', 'feat'), may hold values from -6 to 6
- attn_out: bfloat16 [2, 8192, 2304], P('layer', 'tok', 'feat'), may hold values from -4 to 4
- carry_in: bfloat16 [8192, 2304], P('tok', 'feat'), may hold values from -4 to 4
- enc_weight: bfloat16 [2, 2304, 8192], P('layer', None, 'feat'), may hold values from -0.125 to 0.125
- enc_bias: float32 [2, 8192], P('layer', 'feat'), may hold values from -3 to 3
- dec_own: bfloat16 [2, 8192, 2304], P('layer', 'feat', 'tok'), may hold values from -0.125 to 0.125
- dec_next: bfloat16 [2, 8192, 2304], P('layer', 'feat', 'tok'), may hold values from -0.125 to 0.125
- block_list: int32 [2, 64, 32], P('layer', 'tok'), may hold values from 0 to 63, all different within a row
- block_count: int32 [2, 64], P('layer', 'tok'), may hold values from 8 to 32, as said below
Outputs:
- reconstruction: bfloat16 [2, 8192, 2304], P('layer', 'tok', 'feat')
- outgoing: bfloat16 [2, 8192, 2304], P('layer', 'tok', 'feat')
Inputs may be any that keep to these rules, and one draw needn't show every extreme that they name: Each row of block_list names 32 different blocks; only its first block_count entries are in use. `block_count`: some entry equals 32.
All inputs are finite; a program needn't handle non-finite values.
Results may differ from a plain program's by a relative error of at most 0.015.
Values may be sent and summed in bfloat16 or wider, within the bound.
No kernel may reach another device: no remote copies, remote signals or barrier semaphores. Data moves between devices by JAX's collectives and lax.ppermute only.
A program may use at most 128 MiB of HBM per device.

v0:
```python
import jax
import jax.numpy as jnp
from jax import lax
from jax.sharding import PartitionSpec as P

BLOCK = 128
TILE = 128
GROUP = ("layer", "feat")


def within_layer(shard, section, shift, n_feat):
    if section is None:
        return lax.ppermute(shard, "feat", [(i, (i + shift) % n_feat) for i in range(n_feat)])
    pairs = [(section * n_feat + i, section * n_feat + (i + shift) % n_feat) for i in range(n_feat)]
    return lax.ppermute(shard, GROUP, pairs)


def feat_gather(part, section, feat_index, n_feat):
    received = [part] + [within_layer(part, section, k, n_feat) for k in range(1, n_feat)]
    blocks = []
    for j in range(n_feat):
        block = jnp.zeros_like(part)
        for k in range(n_feat):
            block = jnp.where((feat_index - k) % n_feat == j, received[k], block)
        blocks.append(block)
    return jnp.concatenate(blocks, axis=-1)


def feat_reduce_scatter(terms, section, feat_index, n_feat):
    cols = terms.shape[-1] // n_feat
    total = lax.dynamic_slice_in_dim(terms, feat_index * cols, cols, terms.ndim - 1).astype(
        jnp.float32
    )
    for k in range(1, n_feat):
        target = (feat_index + k) % n_feat
        piece = lax.dynamic_slice_in_dim(terms, target * cols, cols, terms.ndim - 1)
        total = total + within_layer(piece, section, k, n_feat).astype(jnp.float32)
    return total


def decode_scatter(features, decoder, feat_index, n_feat):
    cols = decoder.shape[1] // n_feat
    total = None
    for k in sorted(range(n_feat), key=lambda shift: (-min(shift, n_feat - shift), shift)):
        target = (feat_index + k) % n_feat
        chunk = lax.dynamic_slice_in_dim(decoder, target * cols, cols, 1)
        piece = jnp.dot(features, chunk, preferred_element_type=jnp.float32).astype(jnp.bfloat16)
        if k:
            piece = within_layer(piece, None, k, n_feat)
        else:
            piece = lax.optimization_barrier(piece)
        piece = piece.astype(jnp.float32)
        total = piece if total is None else total + piece
    return total


def feature_mask(block_list, block_count, feat_index, blocks_dev):
    listed = block_list[0]
    in_use = jnp.arange(listed.shape[1], dtype=jnp.int32)[None, :] < block_count[0][:, None]
    own_blocks = feat_index * blocks_dev + jnp.arange(blocks_dev, dtype=jnp.int32)
    matches = (listed[:, None, :] == own_blocks[None, :, None]) & in_use[:, None, :]
    active = jnp.any(matches, axis=2).astype(jnp.float32)
    return jnp.repeat(jnp.repeat(active, TILE, axis=0), BLOCK, axis=1)


def encode(gathered, enc_weight, enc_bias, mask):
    preact = (
        jnp.dot(gathered, enc_weight[0], preferred_element_type=jnp.float32) + enc_bias[0][None, :]
    )
    return (jax.nn.relu(preact) * mask).astype(jnp.bfloat16)


def shards(
    resid_in, attn_out, carry_in, enc_weight, enc_bias, dec_own, dec_next, block_list, block_count
):
    n_feat = lax.axis_size("feat")
    section_index = lax.axis_index("layer")
    feat_index = lax.axis_index("feat")
    blocks_dev = enc_weight.shape[2] // BLOCK
    first_core = section_index == 0
    swapped_next = lax.ppermute(dec_next[0], "layer", [(0, 1), (1, 0)])
    first_dec = jnp.where(first_core, dec_own[0], swapped_next)
    second_dec = jnp.where(first_core, swapped_next, dec_own[0])
    first_full = lax.all_gather(first_dec, "tok", axis=1, tiled=True)
    second_full = lax.all_gather(second_dec, "tok", axis=1, tiled=True)
    mask = feature_mask(block_list, block_count, feat_index, blocks_dev)
    attention = attn_out[0].astype(jnp.float32)
    gathered = feat_gather(resid_in, 0, feat_index, n_feat)
    features = lax.cond(
        first_core,
        lambda source: encode(source, enc_weight, enc_bias, mask),
        lambda source: jnp.zeros((source.shape[0], enc_weight.shape[2]), jnp.bfloat16),
        gathered,
    )
    features = jnp.where(first_core, features, lax.ppermute(features, "layer", [(0, 1)]))
    summed = decode_scatter(features, first_full, feat_index, n_feat)
    recon_first = summed + carry_in.astype(jnp.float32)
    residual_next = (resid_in.astype(jnp.float32) + attention + recon_first).astype(jnp.bfloat16)
    outgoing_first = summed.astype(jnp.bfloat16)
    swapped = lax.ppermute(
        jnp.where(first_core, residual_next, outgoing_first), "layer", [(0, 1), (1, 0)]
    )
    gathered = feat_gather(swapped, 1, feat_index, n_feat)
    features = lax.cond(
        first_core,
        lambda source: jnp.zeros((source.shape[0], enc_weight.shape[2]), jnp.bfloat16),
        lambda source: encode(source, enc_weight, enc_bias, mask),
        gathered,
    )
    features = jnp.where(first_core, lax.ppermute(features, "layer", [(1, 0)]), features)
    summed = decode_scatter(features, second_full, feat_index, n_feat)
    recon_second = summed + outgoing_first.astype(jnp.float32)
    outgoing_second = lax.ppermute(summed.astype(jnp.bfloat16), "layer", [(0, 1)])
    recon_out = jnp.where(first_core, recon_first, recon_second).astype(jnp.bfloat16)
    outgoing_out = jnp.where(first_core, swapped, outgoing_second)
    return (recon_out[None], outgoing_out[None])


def solution(mesh):
    return jax.shard_map(
        shards,
        mesh=mesh,
        in_specs=(
            P("tok", "feat"),
            P("layer", "tok", "feat"),
            P("tok", "feat"),
            P("layer", None, "feat"),
            P("layer", "feat"),
            P("layer", "feat", "tok"),
            P("layer", "feat", "tok"),
            P("layer", "tok", None),
            P("layer", "tok"),
        ),
        out_specs=(P("layer", "tok", "feat"), P("layer", "tok", "feat")),
        check_vma=False,
    )
```

profile of v0, /device:TPU:7, one launch (start us, length us, event | category | flops | bytes accessed | tf_op | source)
XLA Modules:
  0.0 253.3 jit_solution(8539006567864455377)
XLA Ops:
  8.0 1.4 collective-permute-done.4
  9.4 1.8 bitcast_select_fusion
  18.2 1.3 collective-permute-start.3
  19.6 19.7 %collective-permute-done.3 = bf16[256,2048]{1,0:T(8,128)(2,1)} collective-permute-done((bf16[256,2048]{1,0:T(8,128)(2,1)S(1)}, bf16[256,2048]{1,0:T(8,128)(2,1)}, u32[]{:S(2)}, u32[]{:S(2)}) %collective-permute-start.3) | collective-permute-done | bytes 1048608 | tf_op jit(solution)/shard_map/ppermute | solution.py:95
  39.3 2.3 broadcast_select_fusion.1
  41.6 74.9 %all-gather.3.cloned.1.call-done = bf16[2048,2304]{0,1:T(8,128)(2,1)} async-done(((bf16[2048,72]{0,1:T(8,128)(2,1)}), bf16[2048,2304]{0,1:T(8,128)(2,1)}) %all-gather.3.cloned.1.call-update) | async-done | bytes 9437200 | tf_op jit(solution)/shard_map/all_gather | solution.py:84
  116.5 3.6 %fusion.44 = bf16[256,576]{0,1:T(8,128)(2,1)} fusion(bf16[256,2048]{1,0:T(8,128)(2,1)} %broadcast_select_fusion.1, bf16[2048,2304]{0,1:T(8,128)(2,1)} %all-gather.3.cloned.1.call-done, s32[]{:T(128)S(6)} %select_n.357), kind=kOutput, calls=%fused_computation.29 | convolution fusion | flops 604127232 | bytes 3702788 | tf_op jit(solution)/shard_map/dot_general | solution.py:47
  121.3 3.3 %fusion.47 = bf16[256,576]{0,1:T(8,128)(2,1)} fusion(bf16[256,2048]{1,0:T(8,128)(2,1)S(1)} %copy-done.9, bf16[2048,2304]{0,1:T(8,128)(2,1)} %all-gather.3.cloned.1.call-done, s32[]{:T(128)S(6)} %select_n.359), kind=kOutput, calls=%fused_computation.30 | convolution fusion | flops 604127232 | bytes 3702788 | tf_op jit(solution)/shard_map/dot_general | solution.py:47
  124.6 1.8 collective-permute-start.6
  126.4 3.3 %fusion.50 = bf16[256,576]{0,1:T(8,128)(2,1)} fusion(bf16[256,2048]{1,0:T(8,128)(2,1)S(1)} %copy-done.9, bf16[2048,2304]{0,1:T(8,128)(2,1)} %all-gather.3.cloned.1.call-done, s32[]{:T(128)S(6)} %select_n.361), kind=kOutput, calls=%fused_computation.31 | convolution fusion | flops 604127232 | bytes 3702788 | tf_op jit(solution)/shard_map/dot_general | solution.py:47
  129.6 3.0 %fusion.53 = bf16[256,576]{0,1:T(8,128)(2,1)S(1)} fusion(bf16[256,2048]{1,0:T(8,128)(2,1)} %broadcast_select_fusion.1, bf16[2048,2304]{0,1:T(8,128)(2,1)} %all-gather.3.cloned.1.call-done, s32[]{:T(128)S(6)} %select_n.362), kind=kOutput, calls=%fused_computation.32 | convolution fusion | flops 604127232 | bytes 3702788 | tf_op jit(solution)/shard_map/dot_general | solution.py:47
  133.9 3.9 %collective-permute-done.7 = bf16[256,576]{0,1:T(8,128)(2,1)} collective-permute-done((bf16[256,576]{0,1:T(8,128)(2,1)}, bf16[256,576]{0,1:T(8,128)(2,1)}, u32[]{:S(2)}, u32[]{:S(2)}) %collective-permute-start.7) | collective-permute-done | bytes 294944 | tf_op jit(solution)/shard_map/ppermute | solution.py:13
  139.0 2.9 %collective-permute-start.8 = (bf16[256,576]{0,1:T(8,128)(2,1)S(1)}, bf16[256,576]{0,1:T(8,128)(2,1)S(1)}, u32[]{:S(2)}, u32[]{:S(2)}) collective-permute-start(bf16[256,576]{0,1:T(8,128)(2,1)S(1)} %fusion.71), channel_id=1, source_target_pairs={{0,128},{128,0},{1,129},{129,1},{2,130},{130,2},{3,131},{131,3},{4... | collective-permute-start | bytes 884744 | tf_op jit(solution)/shard_map/ppermute | solution.py:100
  143.1 1.9 collective-permute-start.10
  145.1 3.1 %collective-permute-start.11 = (bf16[256,576]{0,1:T(8,128)(2,1)S(1)}, bf16[256,576]{0,1:T(8,128)(2,1)S(1)}, u32[]{:S(2)}, u32[]{:S(2)}) collective-permute-start(bf16[256,576]{0,1:T(8,128)(2,1)S(1)} %collective-permute-done.8), channel_id=1, source_target_pairs={{128,160},{160,192},{192,224},{224,128},{129,161},{161,193},{193,2... | collective-permute-start | bytes 884744 | tf_op jit(solution)/shard_map/ppermute | solution.py:15
  148.1 2.2 collective-permute-start.9
  150.4 1.8 collective-permute-done.10
  152.9 3.9 %collective-permute-done.9 = bf16[256,576]{0,1:T(8,128)(2,1)S(1)} collective-permute-done((bf16[256,576]{0,1:T(8,128)(2,1)S(1)}, bf16[256,576]{0,1:T(8,128)(2,1)S(1)}, u32[]{:S(2)}, u32[]{:S(2)}) %collective-permute-start.9) | collective-permute-done | bytes 294944 | tf_op jit(solution)/shard_map/ppermute | solution.py:15
  157.1 6.5 %conditional.3 = (bf16[256,2048]{1,0:T(8,128)(2,1)S(1)}) conditional(s32[]{:T(128)} %convert_element_type.88, (bf16[1,2304,2048]{2,1,0:T(8,128)(2,1)}, bf16[256,2304]{0,1:T(8,128)(2,1)S(1)}, f32[1,2048]{1,0:T(1,128)S(1)}, f32[256,2048]{1,0:T(8,128)S(1)}) %tuple.46, () %tuple.23), branch_computations={%region_3.4_spmd, %region_4.5_spmd} | conditional | flops 2418016256 | bytes 13770760 | solution.py:104
  157.3 6.3 %fusion.25 = bf16[256,2048]{1,0:T(8,128)(2,1)S(1)} fusion(f32[256,2048]{1,0:T(8,128)S(1)} %get-tuple-element.29, bf16[256,2304]{0,1:T(8,128)(2,1)S(1)} %get-tuple-element.45, bf16[1,2304,2048]{2,1,0:T(8,128)(2,1)} %get-tuple-element.27, f32[2048]{0:T(1024)S(1)} %bitcast.57), kind=kOutput, calls=%fused_computation.11 | convolution fusion | flops 2418016256 | bytes 13770752 | tf_op jit(solution)/shard_map/cond/branch_0_fun/dot_general | solution.py:68
  163.6 1.4 collective-permute-start.12
  165.0 2.2 collective-permute-done.12
  167.3 52.7 %all-gather.5.cloned.1.call-done = bf16[2048,2304]{0,1:T(8,128)(2,1)} async-done(((bf16[2048,72]{0,1:T(8,128)(2,1)}), bf16[2048,2304]{0,1:T(8,128)(2,1)}) %all-gather.5.cloned.1.call-update) | async-done | bytes 9437200 | tf_op jit(solution)/shard_map/all_gather | solution.py:85
  220.0 2.5 fusion.56
  223.7 2.5 fusion.59
  226.2 1.9 collective-permute-start.14
  228.1 2.5 fusion.62
  230.7 2.6 %fusion.65 = bf16[256,576]{0,1:T(8,128)(2,1)S(1)} fusion(bf16[256,2048]{1,0:T(8,128)(2,1)S(1)} %broadcast_select_fusion, bf16[2048,2304]{0,1:T(8,128)(2,1)} %all-gather.5.cloned.1.call-done, s32[]{:T(128)S(6)} %select_n.362), kind=kOutput, calls=%fused_computation.36 | convolution fusion | flops 604127232 | bytes 3702788 | tf_op jit(solution)/shard_map/dot_general | solution.py:47
  233.3 2.2 collective-permute-done.14
  235.4 3.1 %collective-permute-done.15 = bf16[256,576]{0,1:T(8,128)(2,1)S(1)} collective-permute-done((bf16[256,576]{0,1:T(8,128)(2,1)S(1)}, bf16[256,576]{0,1:T(8,128)(2,1)S(1)}, u32[]{:S(2)}, u32[]{:S(2)}) %collective-permute-start.15) | collective-permute-done | bytes 294944 | tf_op jit(solution)/shard_map/ppermute | solution.py:13
  238.5 2.1 fusion.72
  241.9 3.9 %collective-permute-done.16 = bf16[256,576]{0,1:T(8,128)(2,1)S(1)} collective-permute-done((bf16[256,576]{0,1:T(8,128)(2,1)S(1)}, bf16[256,576]{0,1:T(8,128)(2,1)S(1)}, u32[]{:S(2)}, u32[]{:S(2)}) %collective-permute-start.16) | collective-permute-done | bytes 294944 | tf_op jit(solution)/shard_map/ppermute | solution.py:113
  (63 shorter events, 17.2 us)
Async XLA Ops:
  7.2 109.4 %all-gather.3.cloned.1.call-start = ((), (), s32[]{:S(2)}) async-start(), calls=%async_computation | async-start | bytes 9732096 | tf_op jit(solution)/shard_map/all_gather | solution.py:84
  7.2 2.2 collective-permute-start.4
  11.2 208.8 %all-gather.5.cloned.1.call-start = ((), (), s32[]{:S(2)}) async-start(), calls=%async_computation.1 | async-start | bytes 9732096 | tf_op jit(solution)/shard_map/all_gather | solution.py:85
  12.0 5.3 %collective-permute-start = (bf16[256,576]{0,1:T(8,128)(2,1)}, bf16[256,576]{0,1:T(8,128)(2,1)S(1)}, u32[]{:S(2)}, u32[]{:S(2)}) collective-permute-start(bf16[256,576]{0,1:T(8,128)(2,1)} %param.13), channel_id=1, source_target_pairs={{0,96},{32,0},{64,32},{96,64},{1,97},{33,1},{65,33},{97,65},{2,98}... | collective-permute-start | bytes 884744 | tf_op jit(solution)/shard_map/ppermute | solution.py:15
  12.7 4.6 %collective-permute-start.1 = (bf16[256,576]{0,1:T(8,128)(2,1)}, bf16[256,576]{0,1:T(8,128)(2,1)S(1)}, u32[]{:S(2)}, u32[]{:S(2)}) collective-permute-start(bf16[256,576]{0,1:T(8,128)(2,1)} %param.13), channel_id=1, source_target_pairs={{0,64},{32,96},{64,0},{96,32},{1,65},{33,97},{65,1},{97,33},{2,66}... | collective-permute-start | bytes 884744 | tf_op jit(solution)/shard_map/ppermute | solution.py:15
  13.4 3.9 %collective-permute-start.2 = (bf16[256,576]{0,1:T(8,128)(2,1)}, bf16[256,576]{0,1:T(8,128)(2,1)S(1)}, u32[]{:S(2)}, u32[]{:S(2)}) collective-permute-start(bf16[256,576]{0,1:T(8,128)(2,1)} %param.13), channel_id=1, source_target_pairs={{0,32},{32,64},{64,96},{96,0},{1,33},{33,65},{65,97},{97,1},{2,34}... | collective-permute-start | bytes 884744 | tf_op jit(solution)/shard_map/ppermute | solution.py:15
  16.4 1.0 copy-start
  17.4 0.7 copy-start.11
  18.2 21.1 %collective-permute-start.3 = (bf16[256,2048]{1,0:T(8,128)(2,1)S(1)}, bf16[256,2048]{1,0:T(8,128)(2,1)}, u32[]{:S(2)}, u32[]{:S(2)}) collective-permute-start(bf16[256,2048]{1,0:T(8,128)(2,1)S(1)} %get-tuple-element.58), channel_id=1, source_target_pairs={{0,128},{1,129},{2,130},{3,131},{4,132},{5,133},{6,134},{7,135},{8... | collective-permute-start | bytes 3145736 | tf_op jit(solution)/shard_map/ppermute | solution.py:95
  116.5 4.8 %copy-start.9 = (bf16[256,2048]{1,0:T(8,128)(2,1)S(1)}, bf16[256,2048]{1,0:T(8,128)(2,1)}, u32[]{:S(2)}) copy-start(bf16[256,2048]{1,0:T(8,128)(2,1)} %broadcast_select_fusion.1) | copy-start | bytes 3145732
  120.1 12.5 %collective-permute-start.5 = (bf16[256,576]{0,1:T(8,128)(2,1)}, bf16[256,576]{0,1:T(8,128)(2,1)S(1)}, u32[]{:S(2)}, u32[]{:S(2)}) collective-permute-start(bf16[256,576]{0,1:T(8,128)(2,1)} %fusion.44), channel_id=1, source_target_pairs={{0,64},{32,96},{64,0},{96,32},{1,65},{33,97},{65,1},{97,33},{2,66}... | collective-permute-start | bytes 884744 | tf_op jit(solution)/shard_map/ppermute | solution.py:13
  124.6 9.3 %collective-permute-start.6 = (bf16[256,576]{0,1:T(8,128)(2,1)}, bf16[256,576]{0,1:T(8,128)(2,1)S(1)}, u32[]{:S(2)}, u32[]{:S(2)}) collective-permute-start(bf16[256,576]{0,1:T(8,128)(2,1)} %fusion.47), channel_id=1, source_target_pairs={{0,32},{32,64},{64,96},{96,0},{1,33},{33,65},{65,97},{97,1},{2,34}... | collective-permute-start | bytes 884744 | tf_op jit(solution)/shard_map/ppermute | solution.py:13
  129.6 8.1 %copy-start.1 = (bf16[256,576]{0,1:T(8,128)(2,1)S(1)}, bf16[256,576]{0,1:T(8,128)(2,1)}, u32[]{:S(2)}) copy-start(bf16[256,576]{0,1:T(8,128)(2,1)} %param.15) | copy-start | bytes 884740
  129.6 8.1 %collective-permute-start.7 = (bf16[256,576]{0,1:T(8,128)(2,1)}, bf16[256,576]{0,1:T(8,128)(2,1)}, u32[]{:S(2)}, u32[]{:S(2)}) collective-permute-start(bf16[256,576]{0,1:T(8,128)(2,1)} %fusion.50), channel_id=1, source_target_pairs={{0,96},{32,0},{64,32},{96,64},{1,97},{33,1},{65,33},{97,65},{2,98}... | collective-permute-start | bytes 884744 | tf_op jit(solution)/shard_map/ppermute | solution.py:13
  129.6 8.1 %copy-start.10 = (bf16[1,256,576]{1,2,0:T(8,128)(2,1)S(1)}, bf16[1,256,576]{1,2,0:T(8,128)(2,1)}, u32[]{:S(2)}) copy-start(bf16[1,256,576]{1,2,0:T(8,128)(2,1)} %param.14) | copy-start | bytes 884740
  132.6 24.4 %copy-start.7 = (bf16[256,576]{0,1:T(8,128)(2,1)}, bf16[256,576]{0,1:T(8,128)(2,1)S(1)}, u32[]{:S(2)}) copy-start(bf16[256,576]{0,1:T(8,128)(2,1)S(1)} %fusion.53) | copy-start | bytes 884740
  132.6 24.2 %copy-start.3 = (bf16[256,576]{0,1:T(8,128)(2,1)}, bf16[256,576]{0,1:T(8,128)(2,1)S(1)}, u32[]{:S(2)}) copy-start(bf16[256,576]{0,1:T(8,128)(2,1)S(1)} %collective-permute-done.5) | copy-start | bytes 884740
  133.9 22.9 %copy-start.5 = (bf16[256,576]{0,1:T(8,128)(2,1)}, bf16[256,576]{0,1:T(8,128)(2,1)S(1)}, u32[]{:S(2)}) copy-start(bf16[256,576]{0,1:T(8,128)(2,1)S(1)} %collective-permute-done.6) | copy-start | bytes 884740
  139.0 4.1 %collective-permute-start.8 = (bf16[256,576]{0,1:T(8,128)(2,1)S(1)}, bf16[256,576]{0,1:T(8,128)(2,1)S(1)}, u32[]{:S(2)}, u32[]{:S(2)}) collective-permute-start(bf16[256,576]{0,1:T(8,128)(2,1)S(1)} %fusion.71), channel_id=1, source_target_pairs={{0,128},{128,0},{1,129},{129,1},{2,130},{130,2},{3,131},{131,3},{4... | collective-permute-start | bytes 884744 | tf_op jit(solution)/shard_map/ppermute | solution.py:100
  143.1 9.0 %collective-permute-start.10 = (bf16[256,576]{0,1:T(8,128)(2,1)S(1)}, bf16[256,576]{0,1:T(8,128)(2,1)S(1)}, u32[]{:S(2)}, u32[]{:S(2)}) collective-permute-start(bf16[256,576]{0,1:T(8,128)(2,1)S(1)} %collective-permute-done.8), channel_id=1, source_target_pairs={{128,192},{160,224},{192,128},{224,160},{129,193},{161,225},{193,1... | collective-permute-start | bytes 884744 | tf_op jit(solution)/shard_map/ppermute | solution.py:15
  145.1 7.9 %collective-permute-start.11 = (bf16[256,576]{0,1:T(8,128)(2,1)S(1)}, bf16[256,576]{0,1:T(8,128)(2,1)S(1)}, u32[]{:S(2)}, u32[]{:S(2)}) collective-permute-start(bf16[256,576]{0,1:T(8,128)(2,1)S(1)} %collective-permute-done.8), channel_id=1, source_target_pairs={{128,160},{160,192},{192,224},{224,128},{129,161},{161,193},{193,2... | collective-permute-start | bytes 884744 | tf_op jit(solution)/shard_map/ppermute | solution.py:15
  148.1 8.7 %collective-permute-start.9 = (bf16[256,576]{0,1:T(8,128)(2,1)S(1)}, bf16[256,576]{0,1:T(8,128)(2,1)S(1)}, u32[]{:S(2)}, u32[]{:S(2)}) collective-permute-start(bf16[256,576]{0,1:T(8,128)(2,1)S(1)} %collective-permute-done.8), channel_id=1, source_target_pairs={{128,224},{160,128},{192,160},{224,192},{129,225},{161,129},{193,1... | collective-permute-start | bytes 884744 | tf_op jit(solution)/shard_map/ppermute | solution.py:15
  163.6 3.6 %collective-permute-start.12 = (bf16[256,2048]{1,0:T(8,128)(2,1)S(1)}, bf16[256,2048]{1,0:T(8,128)(2,1)S(1)}, u32[]{:S(2)}, u32[]{:S(2)}) collective-permute-start(bf16[256,2048]{1,0:T(8,128)(2,1)S(1)} %get-tuple-element.59), channel_id=1, source_target_pairs={{128,0},{129,1},{130,2},{131,3},{132,4},{133,5},{134,6},{135,7},{1... | collective-permute-start | bytes 3145736 | tf_op jit(solution)/shard_map/ppermute | solution.py:110
  222.5 10.8 %collective-permute-start.13 = (bf16[256,576]{0,1:T(8,128)(2,1)S(1)}, bf16[256,576]{0,1:T(8,128)(2,1)S(1)}, u32[]{:S(2)}, u32[]{:S(2)}) collective-permute-start(bf16[256,576]{0,1:T(8,128)(2,1)S(1)} %fusion.56), channel_id=1, source_target_pairs={{0,64},{32,96},{64,0},{96,32},{1,65},{33,97},{65,1},{97,33},{2,66}... | collective-permute-start | bytes 884744 | tf_op jit(solution)/shard_map/ppermute | solution.py:13
  226.2 9.2 %collective-permute-start.14 = (bf16[256,576]{0,1:T(8,128)(2,1)S(1)}, bf16[256,576]{0,1:T(8,128)(2,1)S(1)}, u32[]{:S(2)}, u32[]{:S(2)}) collective-permute-start(bf16[256,576]{0,1:T(8,128)(2,1)S(1)} %fusion.59), channel_id=1, source_target_pairs={{0,32},{32,64},{64,96},{96,0},{1,33},{33,65},{65,97},{97,1},{2,34}... | collective-permute-start | bytes 884744 | tf_op jit(solution)/shard_map/ppermute | solution.py:13
  230.6 7.9 %copy-start.2 = (bf16[256,576]{0,1:T(8,128)(2,1)S(1)}, bf16[256,576]{0,1:T(8,128)(2,1)}, u32[]{:S(2)}) copy-start(bf16[256,576]{0,1:T(8,128)(2,1)} %param.15) | copy-start | bytes 884740
  230.6 7.9 %copy-start.4 = (bf16[256,576]{0,1:T(8,128)(2,1)S(1)}, bf16[256,576]{0,1:T(8,128)(2,1)}, u32[]{:S(2)}) copy-start(bf16[256,576]{0,1:T(8,128)(2,1)} %copy-done.3) | copy-start | bytes 884740
  230.6 7.9 %copy-start.6 = (bf16[256,576]{0,1:T(8,128)(2,1)S(1)}, bf16[256,576]{0,1:T(8,128)(2,1)}, u32[]{:S(2)}) copy-start(bf16[256,576]{0,1:T(8,128)(2,1)} %copy-done.5) | copy-start | bytes 884740
  230.6 7.9 %copy-start.8 = (bf16[256,576]{0,1:T(8,128)(2,1)S(1)}, bf16[256,576]{0,1:T(8,128)(2,1)}, u32[]{:S(2)}) copy-start(bf16[256,576]{0,1:T(8,128)(2,1)} %copy-done.7) | copy-start | bytes 884740
  230.6 7.9 %collective-permute-start.15 = (bf16[256,576]{0,1:T(8,128)(2,1)S(1)}, bf16[256,576]{0,1:T(8,128)(2,1)S(1)}, u32[]{:S(2)}, u32[]{:S(2)}) collective-permute-start(bf16[256,576]{0,1:T(8,128)(2,1)S(1)} %fusion.62), channel_id=1, source_target_pairs={{0,96},{32,0},{64,32},{96,64},{1,97},{33,1},{65,33},{97,65},{2,98}... | collective-permute-start | bytes 884744 | tf_op jit(solution)/shard_map/ppermute | solution.py:13
  240.6 5.2 %collective-permute-start.16 = (bf16[256,576]{0,1:T(8,128)(2,1)S(1)}, bf16[256,576]{0,1:T(8,128)(2,1)S(1)}, u32[]{:S(2)}, u32[]{:S(2)}) collective-permute-start(bf16[256,576]{0,1:T(8,128)(2,1)S(1)} %get-tuple-element.48), channel_id=1, source_target_pairs={{0,128},{1,129},{2,130},{3,131},{4,132},{5,133},{6,134},{7,135},{8... | collective-permute-start | bytes 884744 | tf_op jit(solution)/shard_map/ppermute | solution.py:113
Sparse Core Ops, SparseCore 0:
  11.4 105.1 all-gather.2
  119.7 100.2 all-gather.4
where the time goes:
time: 254 us; the launch traced here: 253 us
  waiting for transfers between devices  174 us (69%)
  matrix products  29.4 us (12%)
  starting transfers between devices  23.1 us (9%)
  between operations  14.5 us (6%)
  other arithmetic  10.5 us (4%)
    all_gather x1, waiting for transfers between devices, shards(): first_full = lax.all_gather(first_dec, 'tok', axis=1, tiled=True)  74.9 us
    all_gather x1, waiting for transfers between devices, shards(): second_full = lax.all_gather(second_dec, 'tok', axis=1, tiled=True)  52.7 us
    dot_general x8, matrix products, decode_scatter(): jnp.dot(features, chunk, preferred_element_type=jnp.float32)  23.1 us
    ppermute x1, waiting for transfers between devices, shards(): lax.ppermute(features, 'layer', [(0, 1)])  19.7 us
    ppermute x6, waiting for transfers between devices, within_layer(): lax.ppermute(shard, 'feat', [(i, (i + shift) % n_feat) for i in range(n_f...  10.4 us
    ppermute x6, starting transfers between devices, within_layer(): return lax.ppermute(shard, GROUP, pairs)  9.23 us
    ppermute x6, waiting for transfers between devices, within_layer(): return lax.ppermute(shard, GROUP, pairs)  6.48 us
    dot_general x1, matrix products, encode(): jnp.dot(gathered, enc_weight[0], preferred_element_type=jnp.float32)  6.31 us
  transfers between devices with their start and end apart: 19, of which 14 were waited for; matrix products, arithmetic and copies ran while one was open for 14% of the time, Pallas kernels for 0%

commit v1 on v0

--- a/solution.py
+++ b/solution.py
@@ -6,6 +6,14 @@
 BLOCK = 128
 TILE = 128
 GROUP = ("layer", "feat")
+
+
+def _choose_squares(frame, axis_name):
+    w_next = jax.lax.all_to_all(
+        jnp.stack([frame for _ in range(jax.lax.psum(1, axis_name))], axis=0), axis_name, 0, 0
+    )
+    far_arr = jnp.concatenate(w_next, 1)
+    return far_arr
 
 
 def within_layer(shard, section, shift, n_feat):
@@ -82,7 +90,7 @@
     first_dec = jnp.where(first_core, dec_own[0], swapped_next)
     second_dec = jnp.where(first_core, swapped_next, dec_own[0])
     first_full = lax.all_gather(first_dec, "tok", axis=1, tiled=True)
-    second_full = lax.all_gather(second_dec, "tok", axis=1, tiled=True)
+    second_full = _choose_squares(second_dec, "tok")
     mask = feature_mask(block_list, block_count, feat_index, blocks_dev)
     attention = attn_out[0].astype(jnp.float32)
     gathered = feat_gather(resid_in, 0, feat_index, n_feat)

time: 254 us -> 379 us (1.49)
  the two profiles are of different devices: /device:TPU:7 before, /device:TPU:169 now
where the time goes in v1:
time: 379 us
  waiting for transfers between devices  282 us (74%)
  starting transfers between devices  37.2 us (10%)
  matrix products  29.2 us (8%)
  between operations  14.5 us (4%)
  other arithmetic  9.05 us (2%)
  local copies, waits for them, and re-layouts  6.95 us (2%)
    all_gather x1, waiting for transfers between devices, shards(): first_full = lax.all_gather(first_dec, 'tok', axis=1, tiled=True)  233 us
    dot_general x8, matrix products, decode_scatter(): jnp.dot(features, chunk, preferred_element_type=jnp.float32)  22.9 us
    ppermute x1, waiting for transfers between devices, shards(): lax.ppermute(features, 'layer', [(0, 1)])  22 us
    ppermute x6, waiting for transfers between devices, within_layer(): lax.ppermute(shard, 'feat', [(i, (i + shift) % n_feat) for i in range(n_f...  14 us
    ppermute x6, starting transfers between devices, within_layer(): return lax.ppermute(shard, GROUP, pairs)  12.4 us
    all_to_all x1, starting transfers between devices, _choose_squares(): jax.lax.all_to_all(jnp.stack([frame for _ in range(jax.lax.psum(1, axis_n...  9.07 us
    ppermute x6, starting transfers between devices, within_layer(): lax.ppermute(shard, 'feat', [(i, (i + shift) % n_feat) for i in range(n_f...  8.81 us
  transfers between devices with their start and end apart: 19, of which 12 were waited for; matrix products, arithmetic and copies ran while one was open for 9% of the time, Pallas kernels for 0%

profile of v1, /device:TPU:169, one launch (start us, length us, event | category | flops | bytes accessed | tf_op | source)
XLA Modules:
  0.0 378.6 jit_solution(18389020602089908106)
XLA Ops:
  8.0 1.4 collective-permute-done.4
  9.4 1.7 bitcast_select_fusion
  11.1 4.8 %stack.2 = bf16[32,2048,72]{1,2,0:T(8,128)(2,1)} broadcast(bf16[2048,72]{0,1:T(8,128)(2,1)S(1)} %get-tuple-element.64), dimensions={1,2} | broadcast | bytes 9732096 | tf_op jit(solution)/shard_map/stack | solution.py:13
  16.0 9.1 %all-to-all-start = ((bf16[32,2048,72]{1,2,0:T(8,128)(2,1)}), bf16[32,2048,72]{1,2,0:T(8,128)(2,1)}, u32[]{:S(2)}, u32[]{:S(2)}) async-start(bf16[32,2048,72]{1,2,0:T(8,128)(2,1)} %stack.2), calls=%async_computation | async-start | bytes 18874368 | tf_op jit(solution)/shard_map/all_to_all | solution.py:12
  31.3 22.0 %collective-permute-done.3 = bf16[256,2048]{1,0:T(8,128)(2,1)} collective-permute-done((bf16[256,2048]{1,0:T(8,128)(2,1)S(1)}, bf16[256,2048]{1,0:T(8,128)(2,1)}, u32[]{:S(2)}, u32[]{:S(2)}) %collective-permute-start.3) | collective-permute-done | bytes 1048608 | tf_op jit(solution)/shard_map/ppermute | solution.py:103
  53.3 2.4 broadcast_select_fusion.1
  55.7 233.1 %all-gather.2.cloned.1.call-done = bf16[2048,2304]{0,1:T(8,128)(2,1)} async-done(((bf16[2048,72]{0,1:T(8,128)(2,1)}), bf16[2048,2304]{0,1:T(8,128)(2,1)}) %all-gather.2.cloned.1.call-update) | async-done | bytes 9437200 | tf_op jit(solution)/shard_map/all_gather | solution.py:92
  288.8 3.6 fusion.44
  292.4 3.0 collective-permute-start.5
  295.4 3.3 fusion.47
  298.9 3.3 fusion.50
  302.1 2.5 collective-permute-start.7
  304.6 2.8 fusion.53
  307.5 1.7 collective-permute-done.6
  311.5 2.2 collective-permute-start.8
  314.9 1.9 collective-permute-start.11
  316.8 6.5 %collective-permute-start.10 = (bf16[256,576]{0,1:T(8,128)(2,1)S(1)}, bf16[256,576]{0,1:T(8,128)(2,1)S(1)}, u32[]{:S(2)}, u32[]{:S(2)}) collective-permute-start(bf16[256,576]{0,1:T(8,128)(2,1)S(1)} %collective-permute-done.8), channel_id=1, source_target_pairs={{128,192},{160,224},{192,128},{224,160},{129,193},{161,225},{193,1... | collective-permute-start | bytes 884744 | tf_op jit(solution)/shard_map/ppermute | solution.py:23
  323.3 1.9 collective-permute-start.9
  325.2 3.4 collective-permute-done.10
  328.6 2.1 collective-permute-done.9
  331.1 6.3 %conditional.3 = (bf16[256,2048]{1,0:T(8,128)(2,1)S(1)}) conditional(s32[]{:T(128)} %convert_element_type.88, (bf16[1,2304,2048]{2,1,0:T(8,128)(2,1)}, bf16[256,2304]{0,1:T(8,128)(2,1)S(1)}, f32[1,2048]{1,0:T(1,128)S(1)}, f32[256,2048]{1,0:T(8,128)S(1)}) %tuple.46, () %tuple.23), branch_computations={%region_3.4_spmd, %region_4.5_spmd} | conditional | flops 2418016256 | bytes 13770760 | solution.py:112
  331.1 6.3 %fusion.25 = bf16[256,2048]{1,0:T(8,128)(2,1)S(1)} fusion(f32[256,2048]{1,0:T(8,128)S(1)} %get-tuple-element.29, bf16[256,2304]{0,1:T(8,128)(2,1)S(1)} %get-tuple-element.53, bf16[1,2304,2048]{2,1,0:T(8,128)(2,1)} %get-tuple-element.27, f32[2048]{0:T(1024)S(1)} %bitcast.60), kind=kOutput, calls=%fused_computation.11 | convolution fusion | flops 2418016256 | bytes 13770752 | tf_op jit(solution)/shard_map/cond/branch_0_fun/dot_general | solution.py:76
  338.8 2.2 collective-permute-done.12
  341.1 2.5 fusion.62
  343.6 2.5 fusion.59
  346.1 2.5 fusion.56
  349.0 1.8 collective-permute-start.14
  351.7 2.5 fusion.65
  354.2 4.2 %collective-permute-done.13 = bf16[256,576]{0,1:T(8,128)(2,1)S(1)} collective-permute-done((bf16[256,576]{0,1:T(8,128)(2,1)S(1)}, bf16[256,576]{0,1:T(8,128)(2,1)S(1)}, u32[]{:S(2)}, u32[]{:S(2)}) %collective-permute-start.13) | collective-permute-done | bytes 294944 | tf_op jit(solution)/shard_map/ppermute | solution.py:21
  358.4 7.0 %collective-permute-done.14 = bf16[256,576]{0,1:T(8,128)(2,1)S(1)} collective-permute-done((bf16[256,576]{0,1:T(8,128)(2,1)S(1)}, bf16[256,576]{0,1:T(8,128)(2,1)S(1)}, u32[]{:S(2)}, u32[]{:S(2)}) %collective-permute-start.14) | collective-permute-done | bytes 294944 | tf_op jit(solution)/shard_map/ppermute | solution.py:21
  365.5 2.1 fusion.72
  368.8 2.2 collective-permute-done.16
  (67 shorter events, 15.8 us)
Async XLA Ops:
  7.2 281.6 %all-gather.2.cloned.1.call-start = ((), (), s32[]{:S(2)}) async-start(), calls=%async_computation.1 | async-start | bytes 9732096 | tf_op jit(solution)/shard_map/all_gather | solution.py:92
  7.2 2.2 collective-permute-start.4
  16.0 9.1 %copy-start = (bf16[256,576]{0,1:T(8,128)(2,1)S(1)}, bf16[256,576]{0,1:T(8,128)(2,1)}, u32[]{:S(2)}) copy-start(bf16[256,576]{0,1:T(8,128)(2,1)} %param.13) | copy-start | bytes 884740
  16.0 11.3 %copy-start.13 = (s32[1,2]{1,0:T(1,128)S(1)}, s32[1,2]{1,0:T(1,128)}, u32[]{:S(2)}) copy-start(s32[1,2]{1,0:T(1,128)} %param.21) | copy-start | bytes 28
  16.0 11.3 %copy-start.12 = (s32[1,2,32]{2,1,0:T(2,128)S(1)}, s32[1,2,32]{2,1,0:T(2,128)}, u32[]{:S(2)}) copy-start(s32[1,2,32]{2,1,0:T(2,128)} %param.20) | copy-start | bytes 772
  16.0 325.1 %all-to-all-start = ((bf16[32,2048,72]{1,2,0:T(8,128)(2,1)}), bf16[32,2048,72]{1,2,0:T(8,128)(2,1)}, u32[]{:S(2)}, u32[]{:S(2)}) async-start(bf16[32,2048,72]{1,2,0:T(8,128)(2,1)} %stack.2), calls=%async_computation | async-start | bytes 18874368 | tf_op jit(solution)/shard_map/all_to_all | solution.py:12
  25.1 4.0 %collective-permute-start.2 = (bf16[256,576]{0,1:T(8,128)(2,1)S(1)}, bf16[256,576]{0,1:T(8,128)(2,1)S(1)}, u32[]{:S(2)}, u32[]{:S(2)}) collective-permute-start(bf16[256,576]{0,1:T(8,128)(2,1)S(1)} %copy-done), channel_id=1, source_target_pairs={{0,32},{32,64},{64,96},{96,0},{1,33},{33,65},{65,97},{97,1},{2,34}... | collective-permute-start | bytes 884744 | tf_op jit(solution)/shard_map/ppermute | solution.py:23
  25.7 3.3 collective-permute-start.1
  26.4 2.6 collective-permute-start
  29.9 23.4 %collective-permute-start.3 = (bf16[256,2048]{1,0:T(8,128)(2,1)S(1)}, bf16[256,2048]{1,0:T(8,128)(2,1)}, u32[]{:S(2)}, u32[]{:S(2)}) collective-permute-start(bf16[256,2048]{1,0:T(8,128)(2,1)S(1)} %get-tuple-element.66), channel_id=1, source_target_pairs={{0,128},{1,129},{2,130},{3,131},{4,132},{5,133},{6,134},{7,135},{8... | collective-permute-start | bytes 3145736 | tf_op jit(solution)/shard_map/ppermute | solution.py:103
  288.8 6.6 %copy-start.9 = (bf16[256,2048]{1,0:T(8,128)(2,1)S(1)}, bf16[256,2048]{1,0:T(8,128)(2,1)}, u32[]{:S(2)}) copy-start(bf16[256,2048]{1,0:T(8,128)(2,1)} %broadcast_select_fusion.1) | copy-start | bytes 3145732
  292.4 15.1 %collective-permute-start.5 = (bf16[256,576]{0,1:T(8,128)(2,1)}, bf16[256,576]{0,1:T(8,128)(2,1)S(1)}, u32[]{:S(2)}, u32[]{:S(2)}) collective-permute-start(bf16[256,576]{0,1:T(8,128)(2,1)} %fusion.44), channel_id=1, source_target_pairs={{0,64},{32,96},{64,0},{96,32},{1,65},{33,97},{65,1},{97,33},{2,66}... | collective-permute-start | bytes 884744 | tf_op jit(solution)/shard_map/ppermute | solution.py:21
  298.7 10.5 %collective-permute-start.6 = (bf16[256,576]{0,1:T(8,128)(2,1)}, bf16[256,576]{0,1:T(8,128)(2,1)S(1)}, u32[]{:S(2)}, u32[]{:S(2)}) collective-permute-start(bf16[256,576]{0,1:T(8,128)(2,1)} %fusion.47), channel_id=1, source_target_pairs={{0,32},{32,64},{64,96},{96,0},{1,33},{33,65},{65,97},{97,1},{2,34}... | collective-permute-start | bytes 884744 | tf_op jit(solution)/shard_map/ppermute | solution.py:21
  302.1 8.1 %copy-start.1 = (bf16[256,576]{0,1:T(8,128)(2,1)S(1)}, bf16[256,576]{0,1:T(8,128)(2,1)}, u32[]{:S(2)}) copy-start(bf16[256,576]{0,1:T(8,128)(2,1)} %param.15) | copy-start | bytes 884740
  302.1 8.1 %collective-permute-start.7 = (bf16[256,576]{0,1:T(8,128)(2,1)}, bf16[256,576]{0,1:T(8,128)(2,1)}, u32[]{:S(2)}, u32[]{:S(2)}) collective-permute-start(bf16[256,576]{0,1:T(8,128)(2,1)} %fusion.50), channel_id=1, source_target_pairs={{0,96},{32,0},{64,32},{96,64},{1,97},{33,1},{65,33},{97,65},{2,98}... | collective-permute-start | bytes 884744 | tf_op jit(solution)/shard_map/ppermute | solution.py:21
  304.6 5.6 %copy-start.10 = (bf16[1,256,576]{1,2,0:T(8,128)(2,1)S(1)}, bf16[1,256,576]{1,2,0:T(8,128)(2,1)}, u32[]{:S(2)}) copy-start(bf16[1,256,576]{1,2,0:T(8,128)(2,1)} %param.14) | copy-start | bytes 884740
  307.4 23.5 %copy-start.7 = (bf16[256,576]{0,1:T(8,128)(2,1)}, bf16[256,576]{0,1:T(8,128)(2,1)S(1)}, u32[]{:S(2)}) copy-start(bf16[256,576]{0,1:T(8,128)(2,1)S(1)} %fusion.53) | copy-start | bytes 884740
  307.5 23.3 %copy-start.3 = (bf16[256,576]{0,1:T(8,128)(2,1)}, bf16[256,576]{0,1:T(8,128)(2,1)S(1)}, u32[]{:S(2)}) copy-start(bf16[256,576]{0,1:T(8,128)(2,1)S(1)} %collective-permute-done.5) | copy-start | bytes 884740
  309.1 21.6 %copy-start.5 = (bf16[256,576]{0,1:T(8,128)(2,1)}, bf16[256,576]{0,1:T(8,128)(2,1)S(1)}, u32[]{:S(2)}) copy-start(bf16[256,576]{0,1:T(8,128)(2,1)S(1)} %collective-permute-done.6) | copy-start | bytes 884740
  311.5 3.4 collective-permute-start.8
  314.9 10.3 %collective-permute-start.11 = (bf16[256,576]{0,1:T(8,128)(2,1)S(1)}, bf16[256,576]{0,1:T(8,128)(2,1)S(1)}, u32[]{:S(2)}, u32[]{:S(2)}) collective-permute-start(bf16[256,576]{0,1:T(8,128)(2,1)S(1)} %collective-permute-done.8), channel_id=1, source_target_pairs={{128,160},{160,192},{192,224},{224,128},{129,161},{161,193},{193,2... | collective-permute-start | bytes 884744 | tf_op jit(solution)/shard_map/ppermute | solution.py:23
  316.8 11.8 %collective-permute-start.10 = (bf16[256,576]{0,1:T(8,128)(2,1)S(1)}, bf16[256,576]{0,1:T(8,128)(2,1)S(1)}, u32[]{:S(2)}, u32[]{:S(2)}) collective-permute-start(bf16[256,576]{0,1:T(8,128)(2,1)S(1)} %collective-permute-done.8), channel_id=1, source_target_pairs={{128,192},{160,224},{192,128},{224,160},{129,193},{161,225},{193,1... | collective-permute-start | bytes 884744 | tf_op jit(solution)/shard_map/ppermute | solution.py:23
  323.3 7.5 %collective-permute-start.9 = (bf16[256,576]{0,1:T(8,128)(2,1)S(1)}, bf16[256,576]{0,1:T(8,128)(2,1)S(1)}, u32[]{:S(2)}, u32[]{:S(2)}) collective-permute-start(bf16[256,576]{0,1:T(8,128)(2,1)S(1)} %collective-permute-done.8), channel_id=1, source_target_pairs={{128,224},{160,128},{192,160},{224,192},{129,225},{161,129},{193,1... | collective-permute-start | bytes 884744 | tf_op jit(solution)/shard_map/ppermute | solution.py:23
  337.4 3.6 collective-permute-start.12
  348.5 16.9 %copy-start.2 = (bf16[256,576]{0,1:T(8,128)(2,1)S(1)}, bf16[256,576]{0,1:T(8,128)(2,1)}, u32[]{:S(2)}) copy-start(bf16[256,576]{0,1:T(8,128)(2,1)} %param.15) | copy-start | bytes 884740
  348.6 16.9 %copy-start.4 = (bf16[256,576]{0,1:T(8,128)(2,1)S(1)}, bf16[256,576]{0,1:T(8,128)(2,1)}, u32[]{:S(2)}) copy-start(bf16[256,576]{0,1:T(8,128)(2,1)} %copy-done.3) | copy-start | bytes 884740
  348.6 16.9 %copy-start.6 = (bf16[256,576]{0,1:T(8,128)(2,1)S(1)}, bf16[256,576]{0,1:T(8,128)(2,1)}, u32[]{:S(2)}) copy-start(bf16[256,576]{0,1:T(8,128)(2,1)} %copy-done.5) | copy-start | bytes 884740
  348.6 16.9 %copy-start.8 = (bf16[256,576]{0,1:T(8,128)(2,1)S(1)}, bf16[256,576]{0,1:T(8,128)(2,1)}, u32[]{:S(2)}) copy-start(bf16[256,576]{0,1:T(8,128)(2,1)} %copy-done.7) | copy-start | bytes 884740
  348.6 9.8 %collective-permute-start.13 = (bf16[256,576]{0,1:T(8,128)(2,1)S(1)}, bf16[256,576]{0,1:T(8,128)(2,1)S(1)}, u32[]{:S(2)}, u32[]{:S(2)}) collective-permute-start(bf16[256,576]{0,1:T(8,128)(2,1)S(1)} %fusion.56), channel_id=1, source_target_pairs={{0,64},{32,96},{64,0},{96,32},{1,65},{33,97},{65,1},{97,33},{2,66}... | collective-permute-start | bytes 884744 | tf_op jit(solution)/shard_map/ppermute | solution.py:21
  349.0 16.4 %collective-permute-start.14 = (bf16[256,576]{0,1:T(8,128)(2,1)S(1)}, bf16[256,576]{0,1:T(8,128)(2,1)S(1)}, u32[]{:S(2)}, u32[]{:S(2)}) collective-permute-start(bf16[256,576]{0,1:T(8,128)(2,1)S(1)} %fusion.59), channel_id=1, source_target_pairs={{0,32},{32,64},{64,96},{96,0},{1,33},{33,65},{65,97},{97,1},{2,34}... | collective-permute-start | bytes 884744 | tf_op jit(solution)/shard_map/ppermute | solution.py:21
  350.8 14.6 %collective-permute-start.15 = (bf16[256,576]{0,1:T(8,128)(2,1)S(1)}, bf16[256,576]{0,1:T(8,128)(2,1)S(1)}, u32[]{:S(2)}, u32[]{:S(2)}) collective-permute-start(bf16[256,576]{0,1:T(8,128)(2,1)S(1)} %fusion.62), channel_id=1, source_target_pairs={{0,96},{32,0},{64,32},{96,64},{1,97},{33,1},{65,33},{97,65},{2,98}... | collective-permute-start | bytes 884744 | tf_op jit(solution)/shard_map/ppermute | solution.py:21
  367.5 3.5 collective-permute-start.16
  (1 other events, 0.7 us)
Sparse Core Ops, SparseCore 0:
  11.3 277.4 all-gather.1
